TPU v7x, 256 devices: a whole 4x4x8 slice. The times are simulated.
256 devices in a mesh: dict: 16 (over x, z_hi, core), tensor: 16 (over z_lo, y).
Axes of the slice: x: 4, y: 4, z: 8 (z_hi: 2, z_lo: 4; z = z_hi * 4 + z_lo), core: 2. Of those that a mesh axis runs over, the one named last changes fastest.
Arguments:
- residual: bfloat16 [4096, 8192], P('dict', 'tensor'), may hold values from -10 to 10
- norm_gain: float32 [8192], replicated, may hold values from 0.1 to 1.9
- w_query: bfloat16 [8192, 8192], P('dict', 'tensor'), may hold values from -2 to 2
- w_key: bfloat16 [8192, 1024], P('dict'), may hold values from -2 to 2
- value_weight: bfloat16 [8192, 1024], P('dict'), may hold values from -0.0625 to 0.0625
- w_out: bfloat16 [8192, 8192], P('tensor', 'dict'), may hold values from -0.0625 to 0.0625
- decoder: bfloat16 [131072, 8192], P('dict', 'tensor'), may hold values from -0.5 to 0.5
- block_ids: int32 [2], replicated, may hold values from 0 to 1023, as said below
- latent_ids: int32 [4096, 64], P('dict'), may hold values from 0 to 131071, as said below
- latent_vals: float32 [4096, 64], P('dict'), may hold values from 0.5 to 4
- prompt_lens: int32 [16], P('dict'), may hold values from 32 to 256, as said below
Outputs:
- ablations: bfloat16 [2, 4096, 8192], P(None, 'dict', 'tensor')
Inputs may be any that keep to these rules, and one draw needn't show every extreme that they name: `block_ids`: 2 distinct blocks, one of them the last block; block b covers latents b * 128 to b * 128 + 127. `latent_ids`: about half of a row's entries name latents of the swept blocks; a row may name a latent more than once. Prompt p uses its first prompt_lens[p] rows; some prompt uses all 256 and some only 32.
All inputs are finite; a program needn't handle non-finite values.
Results may differ from a plain program's by a relative error of at most 0.009.
Values may be sent and summed in bfloat16 or wider, within the bound.
No kernel may reach another device: no remote copies, remote signals or barrier semaphores. Data moves between devices by JAX's collectives and lax.ppermute only.
A program may use at most 192 MiB of HBM per device.

v0:
```python
import math
import jax
import jax.numpy as jnp
from jax import lax
from jax.sharding import PartitionSpec as P

QUERY_HEADS = 64
KEY_VALUE_HEADS = 8
HEAD_SIZE = 128
BLOCK = 128
PROMPT_ROWS = 256
ABLATION_STEPS = 2
ROPE_BASE = 1000000.0
EPSILON = 1e-06
MASKED = -1e30


def rope_tables(length, head_dim):
    frequency = ROPE_BASE ** (-(jnp.arange(head_dim // 2, dtype=jnp.float32) * 2.0) / head_dim)
    angles = jnp.arange(length, dtype=jnp.float32)[:, None] * frequency[None, :]
    angles = jnp.concatenate([angles, angles], axis=-1)
    return (jnp.cos(angles), jnp.sin(angles))


def apply_rotary(feature_map, cosine_table, sine_table):
    half_width = feature_map.shape[-1] // 2
    first_half = feature_map[..., :half_width]
    second_half = feature_map[..., half_width:]
    turned = jnp.concatenate([-second_half, first_half], axis=-1)
    return feature_map * cosine_table + turned * sine_table


def dense_codes(latent_ids, latent_vals, first_latent):
    offsets = latent_ids - first_latent
    columns = jnp.arange(BLOCK, dtype=jnp.int32)
    matched = offsets[:, :, None] == columns[None, None, :]
    picked = jnp.where(matched, latent_vals[:, :, None], jnp.zeros((), jnp.float32))
    return jnp.sum(picked, axis=1).astype(jnp.bfloat16)


def owner_rows(decoder, block_num):
    lat_count = decoder.shape[0]
    first_latent = block_num * BLOCK
    owner_dict = first_latent // lat_count
    row_offset = first_latent - owner_dict * lat_count
    return (lax.dynamic_slice_in_dim(decoder, row_offset, BLOCK, 0), owner_dict)


DICT = ("dict_x", "dict_z", "core")
DICT_RING = ("dict_z", "core", "dict_x")


def dict_index():
    return (
        lax.axis_index("dict_x") * lax.axis_size("dict_z") + lax.axis_index("dict_z")
    ) * lax.axis_size("core") + lax.axis_index("core")


def dict_size():
    return lax.axis_size("dict_x") * lax.axis_size("dict_z") * lax.axis_size("core")


def butterfly_sum(value, axis, count):
    step = 1
    while step < count:
        pairs = [(i, i ^ step) for i in range(count)]
        value = value + lax.ppermute(value, axis, pairs)
        step *= 2
    return value


def fetch_blocks(decoder, block_ids):
    dict_pos = dict_index()
    dict_count = dict_size()
    blocks = []
    for number in range(ABLATION_STEPS):
        dec_rows, owner_dict = owner_rows(decoder, block_ids[number])
        blocks.append(jnp.where(dict_pos == owner_dict, dec_rows, jnp.zeros_like(dec_rows)))
    held = jnp.stack(blocks)
    step = 1
    while step < dict_count:
        pairs = [(i, i ^ step) for i in range(dict_count)]
        held = held + lax.ppermute(held, DICT, pairs)
        step *= 2
    return held


def body(
    residual,
    norm_gain,
    w_query,
    w_key,
    value_weight,
    w_out,
    decoder,
    block_ids,
    latent_ids,
    latent_vals,
    prompt_lens,
):
    row_count = residual.shape[0]
    col_count = residual.shape[1]
    tensor_pos = lax.axis_index("tensor")
    tensor_count = lax.axis_size("tensor")
    full_width = col_count * tensor_count
    head_cols = w_query.shape[1]
    heads_dev = head_cols // HEAD_SIZE
    query_group_size = QUERY_HEADS // KEY_VALUE_HEADS
    kv_index = tensor_pos * heads_dev // query_group_size
    assert 2 * heads_dev <= query_group_size
    is_key_side = tensor_pos % 2 == 0
    key_cols = lax.dynamic_slice_in_dim(w_key, kv_index * HEAD_SIZE, HEAD_SIZE, 1)
    value_cols = lax.dynamic_slice_in_dim(value_weight, kv_index * HEAD_SIZE, HEAD_SIZE, 1)
    kv_cols = jnp.where(is_key_side, key_cols, value_cols)
    packed = jnp.concatenate([w_query, kv_cols, w_out.T], axis=1)
    ring_gathered = lax.all_gather(packed, DICT_RING, axis=0, tiled=True)
    coef_list = [
        dense_codes(latent_ids, latent_vals, block_ids[number] * BLOCK)
        for number in range(ABLATION_STEPS)
    ]
    col_list = []
    dec_blocks = fetch_blocks(decoder, block_ids)
    for number in range(ABLATION_STEPS):
        dec_slice = dec_blocks[number]
        removed = jnp.dot(coef_list[number], dec_slice, preferred_element_type=jnp.float32)
        col_list.append((residual.astype(jnp.float32) - removed).astype(jnp.bfloat16))
    own_cols = jnp.stack(col_list)
    widened = own_cols.astype(jnp.float32)
    sum_sq = butterfly_sum(
        jnp.sum(widened * widened, axis=-1, keepdims=True), "tensor", tensor_count
    )
    mean_sq = sum_sq / full_width
    gain_cols = lax.dynamic_slice_in_dim(norm_gain, tensor_pos * col_count, col_count)
    normed_cols = (widened * lax.rsqrt(mean_sq + EPSILON) * gain_cols).astype(jnp.bfloat16)
    normed_cols, ring_gathered = lax.optimization_barrier((normed_cols, ring_gathered))
    x_count = lax.axis_size("dict_x")
    z_count = lax.axis_size("dict_z")
    core_count = lax.axis_size("core")
    gathered = ring_gathered.reshape((z_count, core_count, x_count) + packed.shape)
    gathered = jnp.transpose(gathered, (2, 0, 1, 3, 4)).reshape(-1, packed.shape[1])
    normed = lax.all_gather(normed_cols, "tensor", axis=2, tiled=True)
    normed = normed.reshape(ABLATION_STEPS * row_count, full_width)
    qkv_cols = head_cols + HEAD_SIZE
    qkv = jnp.dot(normed, gathered[:, :qkv_cols], preferred_element_type=jnp.float32)
    query_vec = qkv[:, :head_cols]
    kv_vector = qkv[:, head_cols:qkv_cols]
    prompt_count = row_count // PROMPT_ROWS
    cosine_table, sine_table = rope_tables(PROMPT_ROWS, HEAD_SIZE)
    query_vec = apply_rotary(
        query_vec.reshape(ABLATION_STEPS, prompt_count, PROMPT_ROWS, heads_dev, HEAD_SIZE),
        cosine_table[:, None, :],
        sine_table[:, None, :],
    ).astype(jnp.bfloat16)
    kv_vector = kv_vector.reshape(ABLATION_STEPS, prompt_count, PROMPT_ROWS, HEAD_SIZE)
    kv_rotated = apply_rotary(kv_vector, cosine_table, sine_table)
    own_kv = jnp.where(is_key_side, kv_rotated, kv_vector).astype(jnp.bfloat16)
    tensor_pairs = [(i, i ^ 1) for i in range(tensor_count)]
    other_kv = lax.ppermute(own_kv, "tensor", tensor_pairs)
    key_vector = jnp.where(is_key_side, own_kv, other_kv)
    value_vector = jnp.where(is_key_side, other_kv, own_kv)
    positions = jnp.arange(PROMPT_ROWS, dtype=jnp.int32)
    scores = jnp.einsum(
        "spqhd,spkd->sphqk", query_vec, key_vector, preferred_element_type=jnp.float32
    ) / math.sqrt(HEAD_SIZE)
    allowed = (positions[None, None, :] <= positions[None, :, None]) & (
        positions[None, None, :] < prompt_lens[:, None, None]
    )
    scores = jnp.where(allowed[None, :, None, :, :], scores, MASKED)
    weights = jax.nn.softmax(scores, axis=-1).astype(jnp.bfloat16)
    context = jnp.einsum(
        "sphqk,spkd->spqhd", weights, value_vector, preferred_element_type=jnp.float32
    )
    context = context.astype(jnp.bfloat16).reshape(ABLATION_STEPS * row_count, head_cols)
    partial_value = lax.dot_general(
        context,
        gathered[:, qkv_cols:],
        (((1,), (1,)), ((), ())),
        preferred_element_type=jnp.float32,
    ).astype(jnp.bfloat16)
    summed = lax.psum_scatter(
        partial_value.astype(jnp.float32).astype(jnp.bfloat16),
        "tensor",
        scatter_dimension=1,
        tiled=True,
    ).astype(jnp.float32)
    result = own_cols.reshape(ABLATION_STEPS * row_count, col_count).astype(jnp.float32) + summed
    return result.astype(jnp.bfloat16).reshape(ABLATION_STEPS, row_count, col_count)


def solution(mesh):
    dict_count = mesh.shape["dict"]
    core_count = 2 if dict_count % 2 == 0 else 1
    z_count = 2 if dict_count % (2 * core_count) == 0 else 1
    x_count = dict_count // (core_count * z_count)
    devices = mesh.devices.reshape(x_count, z_count, core_count, mesh.shape["tensor"])
    fine = jax.sharding.Mesh(devices, ("dict_x", "dict_z", "core", "tensor"))
    in_specs = (
        P(DICT, "tensor"),
        P(),
        P(DICT, "tensor"),
        P(DICT, None),
        P(DICT, None),
        P("tensor", DICT),
        P(DICT, "tensor"),
        P(),
        P(DICT, None),
        P(DICT, None),
        P(DICT),
    )
    out_specs = P(None, DICT, "tensor")
    return jax.shard_map(body, mesh=fine, in_specs=in_specs, out_specs=out_specs, check_vma=False)
```

profile of v0, /device:TPU:6, one launch (start us, length us, event | category | flops | bytes accessed | tf_op | source)
XLA Modules:
  0.0 456.7 jit_solution(7599784094827931474)
XLA Ops:
  6.5 1.3 copy.67
  7.8 1.0 dynamic-slice_select_fusion
  8.8 2.2 pad_maximum_fusion
  11.1 0.6 fusion.36
  13.0 1.0 select_bitcast_fusion.1
  14.2 1.5 collective-permute-done
  15.8 7.3 %collective-permute-start.1 = (bf16[2,128,512]{2,1,0:T(8,128)(2,1)S(1)}, bf16[2,128,512]{2,1,0:T(8,128)(2,1)S(1)}, u32[]{:S(2)}, u32[]{:S(2)}) collective-permute-start(bf16[2,128,512]{2,1,0:T(8,128)(2,1)S(1)} %fusion.34), channel_id=1, source_target_pairs={{0,32},{16,48},{32,0},{48,16},{64,96},{80,112},{96,64},{112,80},{1... | collective-permute-start | bytes 786440 | tf_op jit(solution)/shard_map/ppermute | solution.py:83
  23.1 16.6 %collective-permute-done.1 = bf16[2,128,512]{2,1,0:T(8,128)(2,1)S(1)} collective-permute-done((bf16[2,128,512]{2,1,0:T(8,128)(2,1)S(1)}, bf16[2,128,512]{2,1,0:T(8,128)(2,1)S(1)}, u32[]{:S(2)}, u32[]{:S(2)}) %collective-permute-start.1) | collective-permute-done | bytes 262176 | tf_op jit(solution)/shard_map/ppermute | solution.py:83
  39.7 1.0 collective-permute-start.2
  41.0 8.9 %collective-permute-done.2 = bf16[2,128,512]{2,1,0:T(8,128)(2,1)S(1)} collective-permute-done((bf16[2,128,512]{2,1,0:T(8,128)(2,1)S(1)}, bf16[2,128,512]{2,1,0:T(8,128)(2,1)S(1)}, u32[]{:S(2)}, u32[]{:S(2)}) %collective-permute-start.2) | collective-permute-done | bytes 262176 | tf_op jit(solution)/shard_map/ppermute | solution.py:83
  50.1 7.8 %select_reduce_fusion.1 = (bf16[256,128]{1,0:T(8,128)(2,1)S(1)}, bf16[256,128]{1,0:T(8,128)(2,1)S(1)}) fusion(f32[256,64]{1,0:T(8,128)S(1)} %copy.65, s32[256,64]{1,0:T(8,128)S(1)} %copy.64, s32[256,64]{1,0:T(8,128)S(1)} %copy.66), kind=kLoop, calls=%fused_computation.6 | loop fusion | flops 12517376 | bytes 327680 | tf_op jit(solution)/shard_map/reduce_sum | solution.py:38
  58.6 2.2 collective-permute-start.4
  60.9 1.6 collective-permute-done.4
  62.4 3.5 collective-permute-start.5
  66.0 1.6 collective-permute-done.5
  67.5 4.9 %collective-permute-start.6 = (f32[2,256,1]{1,0,2:T(2,128)S(1)}, f32[2,256,1]{1,0,2:T(2,128)S(1)}, u32[]{:S(2)}, u32[]{:S(2)}) collective-permute-start(f32[2,256,1]{1,0,2:T(2,128)S(1)} %add.88), channel_id=1, source_target_pairs={{0,4},{1,5},{2,6},{3,7},{4,0},{5,1},{6,2},{7,3},{8,12},{9,13},{10,... | collective-permute-start | bytes 6152 | tf_op jit(solution)/shard_map/ppermute | solution.py:67
  72.4 1.6 collective-permute-done.6
  74.0 3.1 collective-permute-start.7
  77.1 0.8 dynamic_slice.17
  77.8 0.8 collective-permute-done.7
  78.6 1.0 multiply_convert_fusion
  79.6 129.5 %all-gather.3.cloned.1.call-done = bf16[8192,1152]{1,0:T(8,128)(2,1)} async-done(((bf16[512,1152]{1,0:T(8,128)(2,1)}), bf16[8192,1152]{1,0:T(8,128)(2,1)}) %all-gather.3.cloned.1.call-update) | async-done | bytes 18874384 | tf_op jit(solution)/shard_map/all_gather | solution.py:116
  210.8 16.8 %copy.68 = bf16[4,2,2,512,1152]{4,3,2,1,0:T(8,128)(2,1)} copy(bf16[4,2,2,512,1152]{4,3,0,2,1:T(8,128)(2,1)} %bitcast.73) | data formatting | bytes 37748736 | tf_op jit(solution)/shard_map/transpose | solution.py:140
  227.6 81.7 %all-gather.5.cloned.1.call-done = bf16[2,256,8192]{2,1,0:T(8,128)(2,1)} async-done(((bf16[2,256,512]{2,1,0:T(8,128)(2,1)}), bf16[2,256,8192]{2,1,0:T(8,128)(2,1)}) %all-gather.5.cloned.1.call-update) | async-done | bytes 8388624 | tf_op jit(solution)/shard_map/all_gather | solution.py:141
  309.3 14.5 %fusion = f32[512,640]{1,0:T(8,128)S(1)} fusion(bf16[512,8192]{1,0:T(8,128)(2,1)} %bitcast.80, bf16[8192,1152]{1,0:T(8,128)(2,1)} %bitcast.74), kind=kOutput, calls=%fused_computation.1 | convolution fusion | flops 5368709120 | bytes 20185088 | tf_op jit(solution)/shard_map/dot_general | solution.py:144
  324.9 0.6 fusion.35
  325.5 1.6 copy_bitcast_fusion
  327.5 2.1 collective-permute-done.8
  329.6 2.4 fusion.37
  333.2 10.2 %convolution_convert_fusion = bf16[512,8192]{1,0:T(8,128)(2,1)} fusion(bf16[8192,1152]{1,0:T(8,128)(2,1)} %bitcast.75, bf16[64,8,4,128]{3,2,1,0:T(4,128)(2,1)S(1)} %bitcast.78), kind=kOutput, calls=%fused_computation | convolution fusion | flops 4299161600 | bytes 17301504 | tf_op jit(solution)/shard_map/dot_general | solution.py:174
  343.5 104.7 %reduce-scatter.2.cloned.1.call-done = bf16[512,512]{1,0:T(8,128)(2,1)} async-done(((bf16[512,8192]{1,0:T(8,128)(2,1)}), bf16[512,512]{1,0:T(8,128)(2,1)}) %reduce-scatter.2.cloned.1.call-update) | async-done | bytes 524304 | tf_op jit(solution)/shard_map/reduce_scatter | solution.py:180
  448.1 2.0 fusion.13
  (52 shorter events, 5.0 us)
Async XLA Ops:
  6.5 202.6 %all-gather.3.cloned.1.call-start = ((), (), s32[]{:S(2)}) async-start(), calls=%async_computation.1 | async-start | bytes 20054016 | tf_op jit(solution)/shard_map/all_gather | solution.py:116
  6.5 4.5 copy-start.3
  11.0 29.7 %copy-start.1 = (s32[256,64]{0,1:T(8,128)S(1)}, s32[256,64]{0,1:T(8,128)}, u32[]{:S(2)}) copy-start(s32[256,64]{0,1:T(8,128)} %param.19) | copy-start | bytes 196612
  11.0 29.9 %copy-start.2 = (f32[256,64]{0,1:T(8,128)S(1)}, f32[256,64]{0,1:T(8,128)}, u32[]{:S(2)}) copy-start(f32[256,64]{0,1:T(8,128)} %param.20) | copy-start | bytes 196612
  11.0 298.3 %all-gather.5.cloned.1.call-start = ((), (), s32[]{:S(2)}) async-start(), calls=%async_computation.2 | async-start | bytes 8912896 | tf_op jit(solution)/shard_map/all_gather | solution.py:141
  14.1 43.9 %copy-start = (bf16[256,512]{1,0:T(8,128)(2,1)S(1)}, bf16[256,512]{1,0:T(8,128)(2,1)}, u32[]{:S(2)}) copy-start(bf16[256,512]{1,0:T(8,128)(2,1)} %param.11) | copy-start | bytes 786436
  14.1 1.6 collective-permute-start
  15.8 23.9 %collective-permute-start.1 = (bf16[2,128,512]{2,1,0:T(8,128)(2,1)S(1)}, bf16[2,128,512]{2,1,0:T(8,128)(2,1)S(1)}, u32[]{:S(2)}, u32[]{:S(2)}) collective-permute-start(bf16[2,128,512]{2,1,0:T(8,128)(2,1)S(1)} %fusion.34), channel_id=1, source_target_pairs={{0,32},{16,48},{32,0},{48,16},{64,96},{80,112},{96,64},{112,80},{1... | collective-permute-start | bytes 786440 | tf_op jit(solution)/shard_map/ppermute | solution.py:83
  39.7 10.2 %collective-permute-start.2 = (bf16[2,128,512]{2,1,0:T(8,128)(2,1)S(1)}, bf16[2,128,512]{2,1,0:T(8,128)(2,1)S(1)}, u32[]{:S(2)}, u32[]{:S(2)}) collective-permute-start(bf16[2,128,512]{2,1,0:T(8,128)(2,1)S(1)} %fusion.41), channel_id=1, source_target_pairs={{0,64},{16,80},{32,96},{48,112},{64,0},{80,16},{96,32},{112,48},{1... | collective-permute-start | bytes 786440 | tf_op jit(solution)/shard_map/ppermute | solution.py:83
  50.0 8.0 %collective-permute-start.3 = (bf16[2,128,512]{2,1,0:T(8,128)(2,1)S(1)}, bf16[2,128,512]{2,1,0:T(8,128)(2,1)S(1)}, u32[]{:S(2)}, u32[]{:S(2)}) collective-permute-start(bf16[2,128,512]{2,1,0:T(8,128)(2,1)S(1)} %add.84), channel_id=1, source_target_pairs={{0,128},{16,144},{32,160},{48,176},{64,192},{80,208},{96,224},{112... | collective-permute-start | bytes 786440 | tf_op jit(solution)/shard_map/ppermute | solution.py:83
  58.6 3.8 collective-permute-start.4
  62.4 5.1 %collective-permute-start.5 = (f32[2,256,1]{1,0,2:T(2,128)S(1)}, f32[2,256,1]{1,0,2:T(2,128)S(1)}, u32[]{:S(2)}, u32[]{:S(2)}) collective-permute-start(f32[2,256,1]{1,0,2:T(2,128)S(1)} %bitcast_add_fusion.1), channel_id=1, source_target_pairs={{0,2},{1,3},{2,0},{3,1},{4,6},{5,7},{6,4},{7,5},{8,10},{9,11},{10,... | collective-permute-start | bytes 6152 | tf_op jit(solution)/shard_map/ppermute | solution.py:67
  67.5 6.5 %collective-permute-start.6 = (f32[2,256,1]{1,0,2:T(2,128)S(1)}, f32[2,256,1]{1,0,2:T(2,128)S(1)}, u32[]{:S(2)}, u32[]{:S(2)}) collective-permute-start(f32[2,256,1]{1,0,2:T(2,128)S(1)} %add.88), channel_id=1, source_target_pairs={{0,4},{1,5},{2,6},{3,7},{4,0},{5,1},{6,2},{7,3},{8,12},{9,13},{10,... | collective-permute-start | bytes 6152 | tf_op jit(solution)/shard_map/ppermute | solution.py:67
  74.0 4.6 %collective-permute-start.7 = (f32[2,256,1]{1,0,2:T(2,128)S(1)}, f32[2,256,1]{1,0,2:T(2,128)S(1)}, u32[]{:S(2)}, u32[]{:S(2)}) collective-permute-start(f32[2,256,1]{1,0,2:T(2,128)S(1)} %add.89), channel_id=1, source_target_pairs={{0,8},{1,9},{2,10},{3,11},{4,12},{5,13},{6,14},{7,15},{8,0},{9,1},... | collective-permute-start | bytes 6152 | tf_op jit(solution)/shard_map/ppermute | solution.py:67
  209.2 238.9 %reduce-scatter.2.cloned.1.call-start = ((), (), s32[]{:S(2)}) async-start(), calls=%async_computation.3 | async-start | bytes 8912896 | tf_op jit(solution)/shard_map/reduce_scatter | solution.py:180
  324.3 5.3 %collective-permute-start.8 = (bf16[2,1,256,128]{2,3,0,1:T(8,128)(2,1)S(1)}, bf16[2,1,256,128]{2,3,0,1:T(8,128)(2,1)S(1)}, u32[]{:S(2)}, u32[]{:S(2)}) collective-permute-start(bf16[2,1,256,128]{2,3,0,1:T(8,128)(2,1)S(1)} %fusion.21), channel_id=1, source_target_pairs={{0,1},{1,0},{2,3},{3,2},{4,5},{5,4},{6,7},{7,6},{8,9},{9,8},{10,11... | collective-permute-start | bytes 393224 | tf_op jit(solution)/shard_map/ppermute | solution.py:158
Sparse Core Ops, SparseCore 0:
  11.1 197.9 all-gather.2
  210.9 98.3 all-gather.4
  343.5 104.5 reduce-scatter.1
where the time goes:
time: 457 us
  waiting for transfers between devices  351 us (77%)
  matrix products  28.1 us (6%)
  starting transfers between devices  22.5 us (5%)
  local copies, waits for them, and re-layouts  21.8 us (5%)
  other arithmetic  18.2 us (4%)
  between operations  15.4 us (3%)
    all_gather x1, waiting for transfers between devices, body(): ring_gathered = lax.all_gather(packed, DICT_RING, axis=0, tiled=True)  130 us
    reduce_scatter x1, waiting for transfers between devices, body(): lax.psum_scatter(partial_value.astype(jnp.float32).astype(jnp.bfloat16),...  105 us
    all_gather x1, waiting for transfers between devices, body(): normed = lax.all_gather(normed_cols, 'tensor', axis=2, tiled=True)  81.7 us
    ppermute x4, waiting for transfers between devices, fetch_blocks(): held = held + lax.ppermute(held, DICT, pairs)  27 us
    transpose x1, local copies, waits for them, and re-layouts, body(): jnp.transpose(gathered, (2, 0, 1, 3, 4)).reshape(-1, packed.shape[1])  16.8 us
    dot_general x1, matrix products, body(): jnp.dot(normed, gathered[:, :qkv_cols], preferred_element_type=jnp.float32)  14.5 us
    ppermute x4, starting transfers between devices, butterfly_sum(): value = value + lax.ppermute(value, axis, pairs)  13.7 us
    dot_general x1, matrix products, body(): lax.dot_general(context, gathered[:, qkv_cols:], (((1,), (1,)), ((), ()))...  10.2 us
  transfers between devices with their start and end apart: 12, of which 11 were waited for; matrix products, arithmetic and copies ran while one was open for 7% of the time, Pallas kernels for 0%

commit v1 on v0

--- a/solution.py
+++ b/solution.py
@@ -113,7 +113,15 @@
     value_cols = lax.dynamic_slice_in_dim(value_weight, kv_index * HEAD_SIZE, HEAD_SIZE, 1)
     kv_cols = jnp.where(is_key_side, key_cols, value_cols)
     packed = jnp.concatenate([w_query, kv_cols, w_out.T], axis=1)
-    ring_gathered = lax.all_gather(packed, DICT_RING, axis=0, tiled=True)
+    ring_gathered = jnp.concatenate(
+        jax.lax.all_to_all(
+            jnp.stack(jax.lax.psum(1, axis_name=DICT_RING) * [packed]),
+            axis_name=DICT_RING,
+            split_axis=0,
+            concat_axis=0,
+        ),
+        axis=0,
+    )
     coef_list = [
         dense_codes(latent_ids, latent_vals, block_ids[number] * BLOCK)
         for number in range(ABLATION_STEPS)

time: 457 us -> 737 us (1.61)
  waiting for transfers between devices: 351 us -> 617 us
  local copies, waits for them, and re-layouts: 21.8 us -> 35.3 us
    ppermute x4, waiting for transfers between devices: 27 us -> 422 us  [fetch_blocks(): held = held + lax.ppermute(held, DICT, pairs)]
    all_gather x1 -> x0, waiting for transfers between devices: 130 us -> none  [body(): ring_gathered = lax.all_gather(packed, DICT_RING, axis=0, tiled=True)]
    all_to_all x0 -> x1, starting transfers between devices: none -> 11.5 us  [body(): jax.lax.all_to_all(jnp.stack(jax.lax.psum(1, axis_name=DICT_RING) * [pack...]
    ppermute x4, starting transfers between devices: 13.7 us -> 5.66 us  [butterfly_sum(): value = value + lax.ppermute(value, axis, pairs)]
  transfers between devices with their start and end apart: 12 -> 12, of which waited for: 11 -> 10; matrix products, arithmetic and copies ran while one was open for 7% -> 5% of each run, Pallas kernels for 0% -> 0%
where the time goes in v1:
time: 737 us
  waiting for transfers between devices  617 us (84%)
  local copies, waits for them, and re-layouts  35.3 us (5%)
  matrix products  28.5 us (4%)
  starting transfers between devices  25.7 us (3%)
  between operations  15.7 us (2%)
  other arithmetic  14.2 us (2%)
    ppermute x4, waiting for transfers between devices, fetch_blocks(): held = held + lax.ppermute(held, DICT, pairs)  422 us
    reduce_scatter x1, waiting for transfers between devices, body(): lax.psum_scatter(partial_value.astype(jnp.float32).astype(jnp.bfloat16),...  104 us
    all_gather x1, waiting for transfers between devices, body(): normed = lax.all_gather(normed_cols, 'tensor', axis=2, tiled=True)  80.2 us
    transpose x1, local copies, waits for them, and re-layouts, body(): jnp.transpose(gathered, (2, 0, 1, 3, 4)).reshape(-1, packed.shape[1])  16.9 us
  transfers between devices with their start and end apart: 12, of which 10 were waited for; matrix products, arithmetic and copies ran while one was open for 5% of the time, Pallas kernels for 0%

profile of v1, /device:TPU:6, one launch (start us, length us, event | category | flops | bytes accessed | tf_op | source)
XLA Modules:
  0.0 736.8 jit_solution(7227208808920055129)
XLA Ops:
  6.5 1.0 constant_dynamic-slice_fusion
  7.8 1.3 copy.74
  9.9 7.0 stack.20
  16.9 11.5 %all-to-all-start = ((bf16[16,512,1152]{2,1,0:T(8,128)(2,1)}), bf16[16,512,1152]{2,1,0:T(8,128)(2,1)}, u32[]{:S(2)}, u32[]{:S(2)}) async-start(bf16[16,512,1152]{2,1,0:T(8,128)(2,1)} %stack.20), calls=%async_computation | async-start | bytes 37748736 | tf_op jit(solution)/shard_map/all_to_all | solution.py:117
  30.4 1.0 select_bitcast_fusion.1
  31.7 1.4 collective-permute-done
  33.1 5.5 collective-permute-start.1
  38.6 413.8 %collective-permute-done.1 = bf16[2,128,512]{2,1,0:T(8,128)(2,1)S(1)} collective-permute-done((bf16[2,128,512]{2,1,0:T(8,128)(2,1)S(1)}, bf16[2,128,512]{2,1,0:T(8,128)(2,1)S(1)}, u32[]{:S(2)}, u32[]{:S(2)}) %collective-permute-start.1) | collective-permute-done | bytes 262176 | tf_op jit(solution)/shard_map/ppermute | solution.py:83
  452.4 0.9 collective-permute-start.2
  453.7 6.6 collective-permute-done.2
  460.4 1.6 collective-permute-start.3
  461.9 7.8 %select_reduce_fusion.1 = (bf16[256,128]{1,0:T(8,128)(2,1)S(1)}, bf16[256,128]{1,0:T(8,128)(2,1)S(1)}) fusion(f32[256,64]{1,0:T(8,128)S(1)} %copy.70, s32[256,64]{1,0:T(8,128)S(1)} %copy.69, s32[256,64]{1,0:T(8,128)S(1)} %copy.71), kind=kLoop, calls=%fused_computation.6 | loop fusion | flops 12517376 | bytes 327680 | tf_op jit(solution)/shard_map/reduce_sum | solution.py:38
  470.5 1.7 collective-permute-start.4
  472.1 2.0 collective-permute-done.4
  474.1 3.2 collective-permute-start.5
  477.3 1.9 collective-permute-done.5
  479.2 3.6 collective-permute-done.6
  482.8 0.8 collective-permute-start.7
  484.4 2.9 collective-permute-done.7
  487.3 1.0 multiply_convert_fusion
  491.8 16.9 %copy.76 = bf16[4,2,2,512,1152]{4,3,2,1,0:T(8,128)(2,1)} copy(bf16[4,2,2,512,1152]{4,3,0,2,1:T(8,128)(2,1)} %bitcast.15) | data formatting | bytes 37748736 | tf_op jit(solution)/shard_map/transpose | solution.py:148
  508.7 80.2 %all-gather.2.cloned.1.call-done = bf16[2,256,8192]{2,1,0:T(8,128)(2,1)} async-done(((bf16[2,256,512]{2,1,0:T(8,128)(2,1)}), bf16[2,256,8192]{2,1,0:T(8,128)(2,1)}) %all-gather.2.cloned.1.call-update) | async-done | bytes 8388624 | tf_op jit(solution)/shard_map/all_gather | solution.py:149
  588.9 14.5 %fusion = f32[512,640]{1,0:T(8,128)S(1)} fusion(bf16[512,8192]{1,0:T(8,128)(2,1)} %bitcast.82, bf16[8192,1152]{1,0:T(8,128)(2,1)} %bitcast.75), kind=kOutput, calls=%fused_computation.1 | convolution fusion | flops 5368709120 | bytes 20185088 | tf_op jit(solution)/shard_map/dot_general | solution.py:152
  604.5 1.6 fusion.35
  606.5 1.3 copy.113
  607.8 1.4 collective-permute-done.8
  609.3 1.9 fusion.37
  611.5 1.5 fusion.4
  613.2 10.2 %convolution_convert_fusion = bf16[512,8192]{1,0:T(8,128)(2,1)} fusion(bf16[8192,1152]{1,0:T(8,128)(2,1)} %bitcast.76, bf16[64,8,4,128]{3,2,1,0:T(4,128)(2,1)S(1)} %bitcast.79), kind=kOutput, calls=%fused_computation | convolution fusion | flops 4299161600 | bytes 17301504 | tf_op jit(solution)/shard_map/dot_general | solution.py:182
  623.4 0.9 copy-done.1
  624.4 103.5 %reduce-scatter.2.cloned.1.call-done = bf16[512,512]{1,0:T(8,128)(2,1)} async-done(((bf16[512,8192]{1,0:T(8,128)(2,1)}), bf16[512,512]{1,0:T(8,128)(2,1)}) %reduce-scatter.2.cloned.1.call-update) | async-done | bytes 524304 | tf_op jit(solution)/shard_map/reduce_scatter | solution.py:188
  727.9 2.0 fusion.13
  (63 shorter events, 8.7 us)
Async XLA Ops:
  6.5 2.6 copy-start.3
  16.9 11.6 %copy-start.6 = (s32[2]{0:T(128)S(1)}, s32[2]{0:T(128)}, u32[]{:S(2)}) copy-start(s32[2]{0:T(128)} %param.18) | copy-start | bytes 28
  16.9 471.4 %all-to-all-start = ((bf16[16,512,1152]{2,1,0:T(8,128)(2,1)}), bf16[16,512,1152]{2,1,0:T(8,128)(2,1)}, u32[]{:S(2)}, u32[]{:S(2)}) async-start(bf16[16,512,1152]{2,1,0:T(8,128)(2,1)} %stack.20), calls=%async_computation | async-start | bytes 37748736 | tf_op jit(solution)/shard_map/all_to_all | solution.py:117
  28.5 424.9 %copy-start.4 = (s32[256,64]{0,1:T(8,128)S(1)}, s32[256,64]{0,1:T(8,128)}, u32[]{:S(2)}) copy-start(s32[256,64]{0,1:T(8,128)} %param.19) | copy-start | bytes 196612
  28.5 425.1 %copy-start.5 = (f32[256,64]{0,1:T(8,128)S(1)}, f32[256,64]{0,1:T(8,128)}, u32[]{:S(2)}) copy-start(f32[256,64]{0,1:T(8,128)} %param.20) | copy-start | bytes 196612
  28.5 560.4 %all-gather.2.cloned.1.call-start = ((), (), s32[]{:S(2)}) async-start(), calls=%async_computation.2 | async-start | bytes 8912896 | tf_op jit(solution)/shard_map/all_gather | solution.py:149
  31.5 438.4 %copy-start.2 = (bf16[256,512]{1,0:T(8,128)(2,1)S(1)}, bf16[256,512]{1,0:T(8,128)(2,1)}, u32[]{:S(2)}) copy-start(bf16[256,512]{1,0:T(8,128)(2,1)} %param.11) | copy-start | bytes 786436
  31.5 1.6 collective-permute-start
  33.1 419.2 %collective-permute-start.1 = (bf16[2,128,512]{2,1,0:T(8,128)(2,1)S(1)}, bf16[2,128,512]{2,1,0:T(8,128)(2,1)S(1)}, u32[]{:S(2)}, u32[]{:S(2)}) collective-permute-start(bf16[2,128,512]{2,1,0:T(8,128)(2,1)S(1)} %fusion.34), channel_id=1, source_target_pairs={{0,32},{16,48},{32,0},{48,16},{64,96},{80,112},{96,64},{112,80},{1... | collective-permute-start | bytes 786440 | tf_op jit(solution)/shard_map/ppermute | solution.py:83
  452.4 7.9 %collective-permute-start.2 = (bf16[2,128,512]{2,1,0:T(8,128)(2,1)S(1)}, bf16[2,128,512]{2,1,0:T(8,128)(2,1)S(1)}, u32[]{:S(2)}, u32[]{:S(2)}) collective-permute-start(bf16[2,128,512]{2,1,0:T(8,128)(2,1)S(1)} %fusion.41), channel_id=1, source_target_pairs={{0,64},{16,80},{32,96},{48,112},{64,0},{80,16},{96,32},{112,48},{1... | collective-permute-start | bytes 786440 | tf_op jit(solution)/shard_map/ppermute | solution.py:83
  460.4 9.4 %collective-permute-start.3 = (bf16[2,128,512]{2,1,0:T(8,128)(2,1)S(1)}, bf16[2,128,512]{2,1,0:T(8,128)(2,1)S(1)}, u32[]{:S(2)}, u32[]{:S(2)}) collective-permute-start(bf16[2,128,512]{2,1,0:T(8,128)(2,1)S(1)} %add.84), channel_id=1, source_target_pairs={{0,128},{16,144},{32,160},{48,176},{64,192},{80,208},{96,224},{112... | collective-permute-start | bytes 786440 | tf_op jit(solution)/shard_map/ppermute | solution.py:83
  470.3 38.4 %copy-start = (bf16[1,256,512]{2,1,0:T(8,128)(2,1)}, bf16[1,256,512]{2,1,0:T(8,128)(2,1)S(1)}, u32[]{:S(2)}) copy-start(bf16[1,256,512]{2,1,0:T(8,128)(2,1)S(1)} %fusion.7) | copy-start | bytes 786436
  470.5 3.7 collective-permute-start.4
  474.1 5.1 collective-permute-start.5
  479.2 3.6 collective-permute-start.6
  482.8 4.5 collective-permute-start.7
  488.3 239.6 %reduce-scatter.2.cloned.1.call-start = ((), (), s32[]{:S(2)}) async-start(), calls=%async_computation.3 | async-start | bytes 8912896 | tf_op jit(solution)/shard_map/reduce_scatter | solution.py:188
  603.8 5.4 collective-permute-start.8
  623.4 0.9 copy-start.1
Sparse Core Ops, SparseCore 0:
  488.4 100.3 all-gather.1
  623.5 104.3 reduce-scatter.1
